TPU v7x, 512 devices: a whole 4x4x16 slice. The times are simulated.
512 devices in a mesh: req: 32 (over y, x, core), grp: 16 (over z).
Axes of the slice: x: 4, y: 4, z: 16, core: 2. Of those that a mesh axis runs over, the one named last changes fastest.
Arguments:
- normed_token_input: bfloat16 [256, 8192], P(None, 'req'), may hold values from -6 to 6
- key_value_weight: bfloat16 [8192, 2048], P('req', 'grp'), may hold values from -0.0625 to 0.0625
- adapter_down_weight: bfloat16 [8192, 128, 128], P('req', 'grp'), may hold values from -0.0625 to 0.0625
- adapter_up_weight: bfloat16 [128, 64, 2048], P(None, None, 'grp'), may hold values from -0.75 to 0.75
- adapter_index_rows: int32 [256, 1], replicated, may hold values from 0 to 127
- queries: bfloat16 [256, 8192], P('req')
- key_value_pages: bfloat16 [10240, 16, 2, 8, 128], P('req', 'grp')
- lengths: int32 [256], P('req'), may hold values from 0 to 511, as said below
- page_slot_table: int32 [256, 32], P('req'), may hold values from 0 to 255, as said below
- departing_slots: int32 [1024], P('req'), may hold values from 0 to 255, as said below
- departing_target: int32 [1024, 1], P('req'), may hold values from 0 to 31; in each aligned block of 32 rows (0 to 31, 32 to 63, ...) at most 2 rows name the same one
Outputs:
- attention: bfloat16 [256, 8192], P('req')
- migrated_pool: bfloat16 [10240, 16, 2, 8, 128], P('req', 'grp')
Inputs may be any that keep to these rules, and one draw needn't show every extreme that they name: `adapter_index_rows`: each row names one adapter; every adapter is named by some request. `lengths`: some request has an empty cache and some has 511 cached tokens. `page_slot_table`: the rows of the requests of one home together name each of that home's slots 0 .. 255 exactly once. `departing_slots`: the 32 entries of one home are distinct. `departing_target`: the 32 rows of one home name one target at most 2 times; some home names some target exactly 2 times.
All inputs are finite; a program needn't handle non-finite values.
Results may differ from a plain program's by a relative error of at most 0.01345.
Values may be sent and summed in bfloat16 or wider, within the bound.
No kernel may reach another device: no remote copies, remote signals or barrier semaphores. Data moves between devices by JAX's collectives and lax.ppermute only.
A program may use at most 64 MiB of HBM per device.

v0:
```python
import math
import jax
import jax.numpy as jnp
from jax import lax
from jax.sharding import PartitionSpec as P

adapter_scale = 2.0
masked_score = -1e30


def merged_2(part, axis, combine):
    gathered = jax.tree.map(lambda a: lax.all_gather(a, axis), part)

    def take(source):
        return jax.tree.map(lambda a: lax.dynamic_index_in_dim(a, source, 0, False), gathered)

    return lax.fori_loop(
        1, lax.axis_size(axis), lambda source, state: combine(state, take(source)), take(0)
    )


def softmax_join(first, second):
    top = jnp.maximum(first[0], second[0])
    scale_one = jnp.exp(first[0] - top)
    scale_two = jnp.exp(second[0] - top)
    return (
        top,
        first[1] * scale_one + second[1] * scale_two,
        first[2] * scale_one[..., None] + second[2] * scale_two[..., None],
    )


def project_sums(base_part, mid_part):
    return (
        lax.psum_scatter(base_part, "req", scatter_dimension=0, tiled=True),
        lax.psum_scatter(mid_part, "req", scatter_dimension=0, tiled=True),
    )


def shards(
    normed_token_input,
    key_value_weight,
    adapter_down_weight,
    adapter_up_weight,
    adapter_index_rows,
    queries,
    key_value_pages,
    lengths,
    page_slot_table,
    departing_slots,
    departing_target,
):
    selected_adapter = adapter_index_rows[:, 0]
    rank_span_width = adapter_down_weight.shape[2]
    base_part = jnp.dot(normed_token_input, key_value_weight, preferred_element_type=jnp.float32)
    rank_portion = lax.all_gather(adapter_down_weight, "grp", axis=1, tiled=True)
    count = rank_portion.shape[1]
    flat = rank_portion.reshape(rank_portion.shape[0], count * rank_span_width)
    products = jnp.dot(normed_token_input, flat, preferred_element_type=jnp.float32).reshape(
        -1, count, rank_span_width
    )
    picker = (selected_adapter[:, None] == jnp.arange(count, dtype=jnp.int32)[None, :]).astype(
        jnp.float32
    )
    mid_part = jnp.einsum("ia,iaw->iw", picker, products)
    base_resident, mid_home = project_sums(base_part, mid_part)
    rows = lengths.shape[0]
    slot_tokens = key_value_pages.shape[1]
    heads = key_value_pages.shape[3]
    head_dim = key_value_pages.shape[4]
    group_index = lax.axis_index("grp")
    page_size = slot_tokens * lax.axis_size("grp")
    key_width = heads * head_dim
    resident_adapters = lax.dynamic_slice_in_dim(
        selected_adapter, lax.axis_index("req") * rows, rows
    )
    rank_half = adapter_up_weight.shape[1]
    column_span = adapter_up_weight.shape[2]
    mid_cast = mid_home.astype(jnp.bfloat16)
    is_value = group_index * column_span >= key_width
    mid_used = jnp.where(is_value, mid_cast[:, rank_half:], mid_cast[:, :rank_half])
    up_weight_rows = adapter_up_weight[resident_adapters]
    adapter_update = jnp.einsum(
        "ir,irc->ic", mid_used, up_weight_rows, preferred_element_type=jnp.float32
    )
    fresh_columns = (base_resident + adapter_scale * adapter_update).astype(jnp.bfloat16)
    new_all = lax.all_gather(fresh_columns, "grp", axis=1, tiled=True)
    new_keys = new_all[:, :key_width].reshape(rows, heads, head_dim)
    new_values = new_all[:, key_width:].reshape(rows, heads, head_dim)
    request_index = jnp.arange(rows, dtype=jnp.int32)
    page_slot = page_slot_table[request_index, lengths // page_size]
    offset = lengths % page_size
    mine = offset // slot_tokens == group_index
    token_local = offset % slot_tokens
    current = key_value_pages[page_slot, token_local]
    fresh = jnp.stack([new_keys, new_values], axis=1)
    written = key_value_pages.at[page_slot, token_local].set(
        jnp.where(mine[:, None, None, None], fresh, current)
    )
    pages = page_slot_table.shape[1]
    gathered = written[page_slot_table]
    keys = gathered[:, :, :, 0].reshape(rows, pages * slot_tokens, heads, head_dim)
    values = gathered[:, :, :, 1].reshape(rows, pages * slot_tokens, heads, head_dim)
    query = queries.reshape(rows, heads, -1, head_dim)
    scores = jnp.einsum(
        "ihgd,inhd->ihgn", query, keys, preferred_element_type=jnp.float32
    ) / math.sqrt(head_dim)
    positions = (
        jnp.arange(pages, dtype=jnp.int32)[:, None] * page_size
        + group_index * slot_tokens
        + jnp.arange(slot_tokens, dtype=jnp.int32)[None, :]
    ).reshape(-1)
    valid = (positions[None, :] <= lengths[:, None])[:, None, None, :]
    scores = jnp.where(valid, scores, masked_score)
    local_top = jnp.max(scores, axis=3)
    weights = jnp.where(valid, jnp.exp(scores - local_top[..., None]), 0.0)
    local_total = jnp.sum(weights, axis=3)
    local_mixed = jnp.einsum("ihgn,inhd->ihgd", weights, values, preferred_element_type=jnp.float32)
    merged = merged_2((local_top, local_total, local_mixed), "grp", softmax_join)
    total = merged[1]
    mixed = merged[2]
    attention = (mixed / total[..., None]).astype(jnp.bfloat16).reshape(rows, -1)
    targets = departing_target[:, 0]
    count_out = departing_slots.shape[0]
    order = jnp.arange(count_out, dtype=jnp.int32)
    earlier = (targets[:, None] == targets[None, :]) & (order[None, :] < order[:, None])
    place = jnp.sum(earlier.astype(jnp.int32), axis=1)
    live_slots = rows * pages
    home_count = lax.axis_size("req")
    capacity = (key_value_pages.shape[0] - live_slots) // home_count
    outbound = (
        jnp.zeros((home_count, capacity) + key_value_pages.shape[1:], key_value_pages.dtype)
        .at[targets, place]
        .set(written[departing_slots])
    )
    arrived = lax.all_to_all(outbound, "req", split_axis=0, concat_axis=0, tiled=True)
    migrated_pool = jnp.concatenate(
        [
            written[:live_slots],
            arrived.reshape((home_count * capacity,) + key_value_pages.shape[1:]),
        ],
        axis=0,
    )
    return (attention, migrated_pool)


def solution(mesh):
    in_specs = (
        P(None, "req"),
        P("req", "grp"),
        P("req", "grp", None),
        P(None, None, "grp"),
        P(),
        P("req", None),
        P("req", "grp", None, None, None),
        P("req"),
        P("req", None),
        P("req"),
        P("req", None),
    )
    out_specs = (P("req", None), P("req", "grp", None, None, None))
    return jax.shard_map(shards, mesh=mesh, in_specs=in_specs, out_specs=out_specs, check_vma=False)
```

profile of v0, /device:TPU:2, one launch (start us, length us, event | category | flops | bytes accessed | tf_op | source)
XLA Modules:
  0.0 464.8 jit_solution(6286880363566124155)
XLA Ops:
  8.1 1.5 copy.81
  9.6 1.7 fusion.37
  13.2 1.1 gather_fusion
  14.4 1.2 shift-left_bitcast_fusion
  18.2 1.4 fusion.17
  19.6 1.3 dynamic-slice.1
  21.5 1.3 gather_fusion.1
  22.9 1.2 gather_fusion.2
  24.0 120.0 %all-gather.6.cloned.1.call-done = bf16[256,128,128]{2,1,0:T(8,128)(2,1)} async-done(((bf16[256,8,128]{2,1,0:T(8,128)(2,1)}), bf16[256,128,128]{2,1,0:T(8,128)(2,1)}) %all-gather.6.cloned.1.call-update) | async-done | bytes 8388624 | tf_op jit(solution)/shard_map/all_gather | solution.py:56
  144.0 12.8 %copy.40 = bf16[256,128,128]{0,2,1:T(8,128)(2,1)} copy(bf16[256,128,128]{2,1,0:T(8,128)(2,1)} %all-gather.6.cloned.1.call-done) | data formatting | bytes 16777216 | tf_op jit(solution)/shard_map/reshape | solution.py:58
  156.8 11.1 %fusion.5 = bf16[256,128,128]{2,0,1:T(8,128)(2,1)} fusion(bf16[256,128,128]{0,2,1:T(8,128)(2,1)} %copy.40, bf16[256,256]{1,0:T(8,128)(2,1)S(1)} %copy-done.5), kind=kOutput, calls=%fused_computation.17 | convolution fusion | flops 2147483648 | bytes 16908288 | tf_op jit(solution)/shard_map/dot_general | solution.py:59
  167.9 11.1 %fusion.3 = f32[256,1,128]{2,1,0:T(1,128)} fusion(bf16[256,128,128]{2,0,1:T(8,128)(2,1)} %fusion.5, pred[256,128,1]{1,0,2:T(32,128)(4,1)S(1)} %copy-done.8), kind=kOutput, calls=%fused_computation.15 | convolution fusion | flops 8388608 | bytes 8552448 | tf_op jit(solution)/shard_map/ia,iaw->iw/dot_general | solution.py:65
  179.1 119.3 %all-reduce.7 = bf16[256,128]{1,0:T(8,128)(2,1)S(1)} all-reduce(f32[256,128]{1,0:T(8,128)} %bitcast.109), channel_id=6, replica_groups=mesh['req'=32,'grp'=16] {'req'}, use_global_device_ids=true, to_apply=%region_1.0.clone | all-reduce | flops 32768 | bytes 196608
  298.4 1.0 fusion.21
  300.1 28.9 %all_gather.25 = bf16[8,2048]{1,0:T(8,128)(2,1)S(1)} all-gather(bf16[8,128]{1,0:T(8,128)(2,1)S(1)} %fusion.20), channel_id=1, replica_groups=mesh['req'=32,'grp'=16] {'grp'}, dimensions={1}, use_global_device_ids=true | all-gather | bytes 34816 | tf_op jit(solution)/shard_map/all_gather | solution.py:87
  329.2 0.8 scatter_fusion
  330.1 1.8 gather_fusion.3
  331.8 1.3 fusion.35
  334.3 1.0 fusion.9
  335.4 0.9 convert_reduce_fusion
  338.3 3.6 scatter_fusion.1
  341.8 9.8 %all-to-all-start = ((bf16[32,2,1,2,8,128]{5,4,3,1,2,0:T(8,128)(2,1)}), bf16[32,2,1,2,8,128]{5,4,3,1,2,0:T(8,128)(2,1)}, u32[]{:S(2)}, u32[]{:S(2)}) async-start(bf16[32,2,1,2,8,128]{5,4,3,1,2,0:T(8,128)(2,1)} %bitcast.105), calls=%async_computation | async-start | bytes 524288 | tf_op jit(solution)/shard_map/all_to_all | solution.py:136
  351.6 33.6 %all-gather = f32[128,8,8]{2,1,0:T(8,128)S(1)} all-gather(f32[8,8,8]{2,1,0:T(8,128)} %copy-done.6), channel_id=2, replica_groups=mesh['req'=32,'grp'=16] {'grp'}, dimensions={0}, use_global_device_ids=true | all-gather | bytes 34816 | tf_op jit(solution)/shard_map/all_gather | solution.py:12
  385.2 1.4 fusion.11
  386.6 33.6 %all-gather.1 = f32[128,8,8]{2,1,0:T(8,128)S(1)} all-gather(f32[8,8,8]{2,1,0:T(8,128)S(1)} %fusion.11), channel_id=3, replica_groups=mesh['req'=32,'grp'=16] {'grp'}, dimensions={0}, use_global_device_ids=true | all-gather | bytes 34816 | tf_op jit(solution)/shard_map/all_gather | solution.py:12
  421.0 1.1 slice_bitcast_fusion
  422.2 2.5 pad_maximum_fusion
  424.7 1.0 slice.57
  425.6 30.8 %while.19 = (s32[]{:T(128)}, f32[8,8,8]{2,1,0:T(8,128)S(1)}, f32[8,8,8]{2,1,0:T(8,128)S(1)}, f32[8,8,8,128]{3,2,1,0:T(8,128)S(1)}, f32[16,8,8,8]{3,2,1,0:T(8,128...) while((s32[]{:T(128)}, f32[8,8,8]{2,1,0:T(8,128)S(1)}, ...), condition=%wide.region_6.7_spmd, body=%wide.region_5.6_spmd.sunk | while | flops 199685 | bytes 807055 | solution.py:17
  425.7 0.8 fusion.43
  426.5 1.2 fusion.44
  427.7 0.8 fusion.43
  428.5 1.2 fusion.44
  429.8 0.8 fusion.43
  430.6 1.2 fusion.44
  432.7 1.2 fusion.44
  433.9 0.8 fusion.43
  434.7 1.2 fusion.44
  436.8 1.2 fusion.44
  438.8 1.2 fusion.44
  440.9 1.2 fusion.44
  442.9 1.2 fusion.44
  445.0 1.2 fusion.44
  447.0 1.2 fusion.44
  449.1 1.2 fusion.44
  451.2 1.2 fusion.44
  453.2 1.2 fusion.44
  455.3 1.2 fusion.44
  (72 shorter events, 19.4 us)
Async XLA Ops:
  8.0 13.5 %copy-start = (bf16[128,64,128]{2,1,0:T(8,128)(2,1)S(1)}, bf16[128,64,128]{2,1,0:T(8,128)(2,1)}, u32[]{:S(2)}) copy-start(bf16[128,64,128]{2,1,0:T(8,128)(2,1)} %param.16) | copy-start | bytes 6291460
  8.0 1.6 copy-start.5
  8.0 3.9 copy-start.10
  8.0 5.2 %copy-start.1 = (s32[8,32]{1,0:T(8,128)S(1)}, s32[8,32]{1,0:T(8,128)}, u32[]{:S(2)}) copy-start(s32[8,32]{1,0:T(8,128)} %param.21) | copy-start | bytes 3076
  8.0 136.0 %all-gather.6.cloned.1.call-start = ((), (), s32[]{:S(2)}) async-start(), calls=%async_computation.1 | async-start | bytes 8912896 | tf_op jit(solution)/shard_map/all_gather | solution.py:56
  9.6 289.9 %all-reduce.6.cloned.1.call-start = ((), (), s32[]{:S(2)}) async-start(), calls=%async_computation.3 | async-start | bytes 262144
  11.3 413.3 %all-gather.8.cloned.1.call-start = ((), (), s32[]{:S(2)}) async-start(), calls=%async_computation.2 | async-start | bytes 4456448 | tf_op jit(solution)/shard_map/all_gather | solution.py:12
  156.8 11.1 %copy-start.8 = (pred[256,128,1]{1,0,2:T(32,128)(4,1)S(1)}, pred[256,128,1]{1,0,2:T(32,128)(4,1)}, u32[]{:S(2)}) copy-start(pred[256,128,1]{1,0,2:T(32,128)(4,1)} %fusion.17) | copy-start | bytes 98308
  167.9 161.1 %copy-start.7 = (bf16[8,2,8,128]{3,2,1,0:T(8,128)(2,1)S(1)}, bf16[8,2,8,128]{3,2,1,0:T(8,128)(2,1)}, u32[]{:S(2)}) copy-start(bf16[8,2,8,128]{3,2,1,0:T(8,128)(2,1)} %gather_fusion.2) | copy-start | bytes 98308
  167.9 161.2 %copy-start.9 = (pred[8]{0:T(512)(128)(4,1)S(1)}, pred[8]{0:T(512)(128)(4,1)}, u32[]{:S(2)}) copy-start(pred[8]{0:T(512)(128)(4,1)} %fusion.24) | copy-start | bytes 28
  330.0 3.1 copy-start.11
  331.8 3.5 copy-start.12
  333.6 0.7 copy-start.2
  333.6 0.7 copy-start.6
  341.8 80.4 %all-to-all-start = ((bf16[32,2,1,2,8,128]{5,4,3,1,2,0:T(8,128)(2,1)}), bf16[32,2,1,2,8,128]{5,4,3,1,2,0:T(8,128)(2,1)}, u32[]{:S(2)}, u32[]{:S(2)}) async-start(bf16[32,2,1,2,8,128]{5,4,3,1,2,0:T(8,128)(2,1)} %bitcast.105), calls=%async_computation | async-start | bytes 524288 | tf_op jit(solution)/shard_map/all_to_all | solution.py:136
  385.2 1.4 copy-start.3
  420.3 0.8 copy-start.4
Sparse Core Ops, SparseCore 0:
  10.9 133.1 all-gather.5
  335.4 77.9 all-gather.7
Sparse Core Ops, SparseCore 1:
  13.8 136.9 all-reduce.5
where the time goes:
time: 467 us; the launch traced here: 465 us
  blocking collectives  215 us (46%)
  waiting for transfers between devices  120 us (26%)
  other arithmetic  43.3 us (9%)
  local copies, waits for them, and re-layouts  33 us (7%)
  matrix products  26.4 us (6%)
  between operations  16.4 us (4%)
  starting transfers between devices  9.88 us (2%)
    all_gather x1, waiting for transfers between devices, shards(): lax.all_gather(adapter_down_weight, 'grp', axis=1, tiled=True)  120 us
    unnamed x1, blocking collectives  119 us
    all_gather x2, blocking collectives, merged_2(): gathered = jax.tree.map(lambda a: lax.all_gather(a, axis), part)  67.3 us
    all_gather x1, blocking collectives, shards(): new_all = lax.all_gather(fresh_columns, 'grp', axis=1, tiled=True)  28.9 us
    add x15, other arithmetic, softmax_join(): first[2] * scale_one[..., None] + second[2] * scale_two[..., None]  18.2 us
    reshape x1, local copies, waits for them, and re-layouts, shards(): flat = rank_portion.reshape(rank_portion.shape[0], count * rank_span_width)  12.8 us
    add x15, other arithmetic, softmax_join(): first[1] * scale_one + second[1] * scale_two  12.3 us
    dot_general x1, matrix products, shards(): mid_part = jnp.einsum('ia,iaw->iw', picker, products)  11.1 us
  transfers between devices with their start and end apart: 4, of which 1 were waited for; matrix products, arithmetic and copies ran while one was open for 13% of the time, Pallas kernels for 0%

commit v1 on v0

--- a/solution.py
+++ b/solution.py
@@ -6,6 +6,27 @@
 
 adapter_scale = 2.0
 masked_score = -1e30
+
+
+def collect(array, axis, dim):
+    length, index, width = (lax.axis_size(axis), lax.axis_index(axis), array.shape[dim])
+    right = [(i, (i + 1) % length) for i in range(length)]
+    left = [(i, (i - 1) % length) for i in range(length)]
+    out = jnp.zeros((*array.shape[:dim], length * width, *array.shape[dim + 1 :]), array.dtype)
+    out = lax.dynamic_update_slice_in_dim(out, array, index * width, axis=dim)
+    from_left = from_right = array
+    half = length // 2
+    for lap in range(1, half + 1):
+        from_left = lax.ppermute(from_left, axis, right)
+        out = lax.dynamic_update_slice_in_dim(
+            out, from_left, (index - lap) % length * width, axis=dim
+        )
+        if lap < length - half:
+            from_right = lax.ppermute(from_right, axis, left)
+            out = lax.dynamic_update_slice_in_dim(
+                out, from_right, (index + lap) % length * width, axis=dim
+            )
+    return out
 
 
 def merged_2(part, axis, combine):
@@ -53,7 +74,7 @@
     selected_adapter = adapter_index_rows[:, 0]
     rank_span_width = adapter_down_weight.shape[2]
     base_part = jnp.dot(normed_token_input, key_value_weight, preferred_element_type=jnp.float32)
-    rank_portion = lax.all_gather(adapter_down_weight, "grp", axis=1, tiled=True)
+    rank_portion = collect(adapter_down_weight, "grp", 1)
     count = rank_portion.shape[1]
     flat = rank_portion.reshape(rank_portion.shape[0], count * rank_span_width)
     products = jnp.dot(normed_token_input, flat, preferred_element_type=jnp.float32).reshape(

time: 467 us -> 473 us (1.013)
  the two profiles are of different devices: /device:TPU:2 before, /device:TPU:16 now
where the time goes in v1:
time: 473 us; the launch traced here: 470 us
  blocking collectives  199 us (42%)
  starting transfers between devices  82.3 us (17%)
  local copies, waits for them, and re-layouts  63.7 us (13%)
  other arithmetic  40.4 us (9%)
  matrix products  35.3 us (7%)
  waiting for transfers between devices  33.8 us (7%)
  between operations  15.3 us (3%)
    unnamed x1, blocking collectives  105 us
    all_gather x2, blocking collectives, merged_2(): gathered = jax.tree.map(lambda a: lax.all_gather(a, axis), part)  67.6 us
    ppermute x7, starting transfers between devices, collect(): from_right = lax.ppermute(from_right, axis, left)  40.7 us
    ppermute x8, waiting for transfers between devices, collect(): from_left = lax.ppermute(from_left, axis, right)  33.2 us
    all_gather x1, blocking collectives, shards(): new_all = lax.all_gather(fresh_columns, 'grp', axis=1, tiled=True)  26.1 us
    all_to_all x1, starting transfers between devices, shards(): lax.all_to_all(outbound, 'req', split_axis=0, concat_axis=0, tiled=True)  24.2 us
    dot_general x1, matrix products, shards(): jnp.dot(normed_token_input, flat, preferred_element_type=jnp.float32)  23.8 us
    add x15, other arithmetic, softmax_join(): first[2] * scale_one[..., None] + second[2] * scale_two[..., None]  18.2 us
  transfers between devices with their start and end apart: 18, of which 7 were waited for; matrix products, arithmetic and copies ran while one was open for 20% of the time, Pallas kernels for 0%

profile of v1, /device:TPU:16, one launch (start us, length us, event | category | flops | bytes accessed | tf_op | source)
XLA Modules:
  0.0 469.8 jit_solution(15546760080448728901)
XLA Ops:
  7.2 1.5 copy.97
  8.7 3.8 collective-permute-start
  12.5 9.5 %collective-permute-start.1 = (bf16[256,8,128]{2,1,0:T(8,128)(2,1)}, bf16[256,8,128]{2,1,0:T(8,128)(2,1)}, u32[]{:S(2)}, u32[]{:S(2)}) collective-permute-start(bf16[256,8,128]{2,1,0:T(8,128)(2,1)} %param.15), channel_id=1, source_target_pairs={{0,15},{1,0},{2,1},{3,2},{4,3},{5,4},{6,5},{7,6},{8,7},{9,8},{10,9... | collective-permute-start | bytes 1572872 | tf_op jit(solution)/shard_map/ppermute | solution.py:25
  22.0 10.3 %collective-permute-done = bf16[256,8,128]{2,1,0:T(8,128)(2,1)} collective-permute-done((bf16[256,8,128]{2,1,0:T(8,128)(2,1)}, bf16[256,8,128]{2,1,0:T(8,128)(2,1)}, u32[]{:S(2)}, u32[]{:S(2)}) %collective-permute-start) | collective-permute-done | bytes 524320 | tf_op jit(solution)/shard_map/ppermute | solution.py:20
  32.3 1.9 collective-permute-start.2
  34.3 5.1 %collective-permute-start.3 = (bf16[256,8,128]{2,1,0:T(8,128)(2,1)}, bf16[256,8,128]{2,1,0:T(8,128)(2,1)}, u32[]{:S(2)}, u32[]{:S(2)}) collective-permute-start(bf16[256,8,128]{2,1,0:T(8,128)(2,1)} %collective-permute-done.1), channel_id=1, source_target_pairs={{0,15},{1,0},{2,1},{3,2},{4,3},{5,4},{6,5},{7,6},{8,7},{9,8},{10,9... | collective-permute-start | bytes 1572872 | tf_op jit(solution)/shard_map/ppermute | solution.py:25
  39.4 1.7 fusion.36
  41.2 7.6 %collective-permute-done.2 = bf16[256,8,128]{2,1,0:T(8,128)(2,1)} collective-permute-done((bf16[256,8,128]{2,1,0:T(8,128)(2,1)}, bf16[256,8,128]{2,1,0:T(8,128)(2,1)}, u32[]{:S(2)}, u32[]{:S(2)}) %collective-permute-start.2) | collective-permute-done | bytes 524320 | tf_op jit(solution)/shard_map/ppermute | solution.py:20
  48.8 1.9 collective-permute-start.4
  51.5 5.1 %collective-permute-start.5 = (bf16[256,8,128]{2,1,0:T(8,128)(2,1)}, bf16[256,8,128]{2,1,0:T(8,128)(2,1)}, u32[]{:S(2)}, u32[]{:S(2)}) collective-permute-start(bf16[256,8,128]{2,1,0:T(8,128)(2,1)} %collective-permute-done.3), channel_id=1, source_target_pairs={{0,15},{1,0},{2,1},{3,2},{4,3},{5,4},{6,5},{7,6},{8,7},{9,8},{10,9... | collective-permute-start | bytes 1572872 | tf_op jit(solution)/shard_map/ppermute | solution.py:25
  57.3 1.3 gather_fusion
  58.6 5.8 %collective-permute-done.4 = bf16[256,8,128]{2,1,0:T(8,128)(2,1)} collective-permute-done((bf16[256,8,128]{2,1,0:T(8,128)(2,1)}, bf16[256,8,128]{2,1,0:T(8,128)(2,1)}, u32[]{:S(2)}, u32[]{:S(2)}) %collective-permute-start.4) | collective-permute-done | bytes 524320 | tf_op jit(solution)/shard_map/ppermute | solution.py:20
  64.5 1.9 collective-permute-start.6
  67.8 5.1 %collective-permute-start.7 = (bf16[256,8,128]{2,1,0:T(8,128)(2,1)}, bf16[256,8,128]{2,1,0:T(8,128)(2,1)}, u32[]{:S(2)}, u32[]{:S(2)}) collective-permute-start(bf16[256,8,128]{2,1,0:T(8,128)(2,1)} %collective-permute-done.5), channel_id=1, source_target_pairs={{0,15},{1,0},{2,1},{3,2},{4,3},{5,4},{6,5},{7,6},{8,7},{9,8},{10,9... | collective-permute-start | bytes 1572872 | tf_op jit(solution)/shard_map/ppermute | solution.py:25
  72.9 5.4 %broadcast_in_dim.69 = bf16[256,128,128]{2,1,0:T(8,128)(2,1)} broadcast(bf16[]{:T(256)} %constant.211.clone.1), dimensions={} | broadcast | bytes 8388610 | tf_op jit(solution)/shard_map/broadcast_in_dim | solution.py:15
  79.3 1.9 collective-permute-start.8
  81.9 5.6 %collective-permute-start.9 = (bf16[256,8,128]{2,1,0:T(8,128)(2,1)}, bf16[256,8,128]{2,1,0:T(8,128)(2,1)}, u32[]{:S(2)}, u32[]{:S(2)}) collective-permute-start(bf16[256,8,128]{2,1,0:T(8,128)(2,1)} %collective-permute-done.7), channel_id=1, source_target_pairs={{0,15},{1,0},{2,1},{3,2},{4,3},{5,4},{6,5},{7,6},{8,7},{9,8},{10,9... | collective-permute-start | bytes 1572872 | tf_op jit(solution)/shard_map/ppermute | solution.py:25
  87.5 5.9 %collective-permute-done.8 = bf16[256,8,128]{2,1,0:T(8,128)(2,1)} collective-permute-done((bf16[256,8,128]{2,1,0:T(8,128)(2,1)}, bf16[256,8,128]{2,1,0:T(8,128)(2,1)}, u32[]{:S(2)}, u32[]{:S(2)}) %collective-permute-start.8) | collective-permute-done | bytes 524320 | tf_op jit(solution)/shard_map/ppermute | solution.py:20
  93.4 1.9 collective-permute-start.10
  99.4 2.0 constant_dynamic-update-slice_fusion.14
  101.4 1.9 constant_dynamic-update-slice_fusion.13
  103.3 1.9 constant_dynamic-update-slice_fusion.12
  105.2 5.1 %collective-permute-start.11 = (bf16[256,8,128]{2,1,0:T(8,128)(2,1)}, bf16[256,8,128]{2,1,0:T(8,128)(2,1)S(1)}, u32[]{:S(2)}, u32[]{:S(2)}) collective-permute-start(bf16[256,8,128]{2,1,0:T(8,128)(2,1)} %collective-permute-done.9), channel_id=1, source_target_pairs={{0,15},{1,0},{2,1},{3,2},{4,3},{5,4},{6,5},{7,6},{8,7},{9,8},{10,9... | collective-permute-start | bytes 1572872 | tf_op jit(solution)/shard_map/ppermute | solution.py:25
  110.3 2.0 constant_dynamic-update-slice_fusion.11
  112.3 1.9 collective-permute-start.12
  114.2 1.9 constant_dynamic-update-slice_fusion.10
  116.1 1.9 constant_dynamic-update-slice_fusion.9
  118.1 1.9 constant_dynamic-update-slice_fusion.8
  120.0 2.0 constant_dynamic-update-slice_fusion.7
  122.0 5.1 %collective-permute-start.13 = (bf16[256,8,128]{2,1,0:T(8,128)(2,1)S(1)}, bf16[256,8,128]{2,1,0:T(8,128)(2,1)S(1)}, u32[]{:S(2)}, u32[]{:S(2)}) collective-permute-start(bf16[256,8,128]{2,1,0:T(8,128)(2,1)S(1)} %collective-permute-done.11), channel_id=1, source_target_pairs={{0,15},{1,0},{2,1},{3,2},{4,3},{5,4},{6,5},{7,6},{8,7},{9,8},{10,9... | collective-permute-start | bytes 1572872 | tf_op jit(solution)/shard_map/ppermute | solution.py:25
  127.1 2.0 constant_dynamic-update-slice_fusion.6
  129.1 2.1 collective-permute-start.14
  131.2 1.9 constant_dynamic-update-slice_fusion.5
  133.1 2.0 constant_dynamic-update-slice_fusion.4
  137.9 3.5 collective-permute-done.14
  142.3 23.8 %fusion.3 = bf16[16384,256]{1,0:T(8,128)(2,1)} fusion(bf16[256,256]{1,0:T(8,128)(2,1)S(1)} %copy-done.4, bf16[32,8,128,128]{3,2,1,0:T(8,128)(2,1)} %bitcast.39), kind=kOutput, calls=%fused_computation.15 | convolution fusion | flops 2147483648 | bytes 16908288 | tf_op jit(solution)/shard_map/dot_general | solution.py:80
  166.1 12.5 %copy.34 = bf16[256,128,128]{2,1,0:T(8,128)(2,1)} copy(bf16[256,128,128]{0,2,1:T(8,128)(2,1)} %bitcast.100) | data formatting | bytes 16777216 | tf_op jit(solution)/shard_map/reshape | solution.py:80
  178.6 6.3 %fusion.9 = f32[256,1,128]{2,1,0:T(1,128)} fusion(bf16[256,128,128]{2,1,0:T(8,128)(2,1)} %copy.34, pred[256,128,1]{1,0,2:T(32,128)(4,1)S(1)} %fusion.16), kind=kOutput, calls=%fused_computation.26 | convolution fusion | flops 8388608 | bytes 8552448 | tf_op jit(solution)/shard_map/ia,iaw->iw/dot_general | solution.py:86
  184.9 105.0 %all-reduce.7 = bf16[256,128]{1,0:T(8,128)(2,1)S(1)} all-reduce(f32[256,128]{1,0:T(8,128)} %bitcast.107), channel_id=6, replica_groups=mesh['req'=32,'grp'=16] {'req'}, use_global_device_ids=true, to_apply=%region_1.2.clone | all-reduce | flops 32768 | bytes 196608
  291.7 26.1 %all_gather.21 = bf16[8,2048]{1,0:T(8,128)(2,1)S(1)} all-gather(bf16[8,128]{1,0:T(8,128)(2,1)S(1)} %fusion.19), channel_id=1, replica_groups=mesh['req'=32,'grp'=16] {'grp'}, dimensions={1}, use_global_device_ids=true | all-gather | bytes 34816 | tf_op jit(solution)/shard_map/all_gather | solution.py:108
  318.7 1.8 gather_fusion.3
  321.7 1.4 fusion.35
  328.4 3.6 scatter_fusion.1
  332.0 24.2 %all-to-all-start = ((bf16[32,2,1,2,8,128]{5,4,3,1,2,0:T(8,128)(2,1)}), bf16[32,2,1,2,8,128]{5,4,3,1,2,0:T(8,128)(2,1)}, u32[]{:S(2)}, u32[]{:S(2)}) async-start(bf16[32,2,1,2,8,128]{5,4,3,1,2,0:T(8,128)(2,1)} %bitcast.103), calls=%async_computation | async-start | bytes 524288 | tf_op jit(solution)/shard_map/all_to_all | solution.py:157
  357.4 35.9 %all-gather.1 = f32[128,8,8]{2,1,0:T(8,128)S(1)} all-gather(f32[8,8,8]{2,1,0:T(8,128)S(1)} %fusion.11), channel_id=3, replica_groups=mesh['req'=32,'grp'=16] {'grp'}, dimensions={0}, use_global_device_ids=true | all-gather | bytes 34816 | tf_op jit(solution)/shard_map/all_gather | solution.py:33
  394.1 31.7 %all-gather = f32[128,8,8]{2,1,0:T(8,128)S(1)} all-gather(f32[8,8,8]{2,1,0:T(8,128)} %copy-done.6), channel_id=2, replica_groups=mesh['req'=32,'grp'=16] {'grp'}, dimensions={0}, use_global_device_ids=true | all-gather | bytes 34816 | tf_op jit(solution)/shard_map/all_gather | solution.py:33
  427.8 2.5 pad_maximum_fusion
  431.3 30.8 %while.19 = (s32[]{:T(128)}, f32[8,8,8]{2,1,0:T(8,128)S(1)}, f32[8,8,8]{2,1,0:T(8,128)S(1)}, f32[8,8,8,128]{3,2,1,0:T(8,128)S(1)}, f32[16,8,8,8]{3,2,1,0:T(8,128...) while((s32[]{:T(128)}, f32[8,8,8]{2,1,0:T(8,128)S(1)}, ...), condition=%wide.region_6.7_spmd, body=%wide.region_5.6_spmd.sunk | while | flops 199685 | bytes 807063 | solution.py:38
  (107 shorter events, 57.0 us)
Async XLA Ops:
  7.2 90.4 %copy-start = (bf16[128,64,128]{2,1,0:T(8,128)(2,1)S(1)}, bf16[128,64,128]{2,1,0:T(8,128)(2,1)}, u32[]{:S(2)}) copy-start(bf16[128,64,128]{2,1,0:T(8,128)(2,1)} %param.16) | copy-start | bytes 6291460
  7.2 74.0 %copy-start.7 = (s32[256,1]{0,1:T(1,128)S(1)}, s32[256,1]{0,1:T(1,128)}, u32[]{:S(2)}) copy-start(s32[256,1]{0,1:T(1,128)} %param.17) | copy-start | bytes 3076
  7.2 74.0 %copy-start.8 = (s32[8]{0:T(128)S(1)}, s32[8]{0:T(128)}, u32[]{:S(2)}) copy-start(s32[8]{0:T(128)} %param.20) | copy-start | bytes 100
  7.2 283.8 %all-reduce.6.cloned.1.call-start = ((), (), s32[]{:S(2)}) async-start(), calls=%async_computation.2 | async-start | bytes 262144
  8.7 23.6 %collective-permute-start = (bf16[256,8,128]{2,1,0:T(8,128)(2,1)}, bf16[256,8,128]{2,1,0:T(8,128)(2,1)}, u32[]{:S(2)}, u32[]{:S(2)}) collective-permute-start(bf16[256,8,128]{2,1,0:T(8,128)(2,1)} %param.15), channel_id=1, source_target_pairs={{0,1},{1,2},{2,3},{3,4},{4,5},{5,6},{6,7},{7,8},{8,9},{9,10},{10,1... | collective-permute-start | bytes 1572872 | tf_op jit(solution)/shard_map/ppermute | solution.py:20
  12.5 21.7 %collective-permute-start.1 = (bf16[256,8,128]{2,1,0:T(8,128)(2,1)}, bf16[256,8,128]{2,1,0:T(8,128)(2,1)}, u32[]{:S(2)}, u32[]{:S(2)}) collective-permute-start(bf16[256,8,128]{2,1,0:T(8,128)(2,1)} %param.15), channel_id=1, source_target_pairs={{0,15},{1,0},{2,1},{3,2},{4,3},{5,4},{6,5},{7,6},{8,7},{9,8},{10,9... | collective-permute-start | bytes 1572872 | tf_op jit(solution)/shard_map/ppermute | solution.py:25
  32.3 16.5 %collective-permute-start.2 = (bf16[256,8,128]{2,1,0:T(8,128)(2,1)}, bf16[256,8,128]{2,1,0:T(8,128)(2,1)}, u32[]{:S(2)}, u32[]{:S(2)}) collective-permute-start(bf16[256,8,128]{2,1,0:T(8,128)(2,1)} %collective-permute-done), channel_id=1, source_target_pairs={{0,1},{1,2},{2,3},{3,4},{4,5},{5,6},{6,7},{7,8},{8,9},{9,10},{10,1... | collective-permute-start | bytes 1572872 | tf_op jit(solution)/shard_map/ppermute | solution.py:20
  34.3 17.2 %collective-permute-start.3 = (bf16[256,8,128]{2,1,0:T(8,128)(2,1)}, bf16[256,8,128]{2,1,0:T(8,128)(2,1)}, u32[]{:S(2)}, u32[]{:S(2)}) collective-permute-start(bf16[256,8,128]{2,1,0:T(8,128)(2,1)} %collective-permute-done.1), channel_id=1, source_target_pairs={{0,15},{1,0},{2,1},{3,2},{4,3},{5,4},{6,5},{7,6},{8,7},{9,8},{10,9... | collective-permute-start | bytes 1572872 | tf_op jit(solution)/shard_map/ppermute | solution.py:25
  41.2 389.2 %all-gather.5.cloned.1.call-start = ((), (), s32[]{:S(2)}) async-start(), calls=%async_computation.1 | async-start | bytes 4456448 | tf_op jit(solution)/shard_map/all_gather | solution.py:33
  48.8 15.6 %collective-permute-start.4 = (bf16[256,8,128]{2,1,0:T(8,128)(2,1)}, bf16[256,8,128]{2,1,0:T(8,128)(2,1)}, u32[]{:S(2)}, u32[]{:S(2)}) collective-permute-start(bf16[256,8,128]{2,1,0:T(8,128)(2,1)} %collective-permute-done.2), channel_id=1, source_target_pairs={{0,1},{1,2},{2,3},{3,4},{4,5},{5,6},{6,7},{7,8},{8,9},{9,10},{10,1... | collective-permute-start | bytes 1572872 | tf_op jit(solution)/shard_map/ppermute | solution.py:20
  51.5 16.3 %collective-permute-start.5 = (bf16[256,8,128]{2,1,0:T(8,128)(2,1)}, bf16[256,8,128]{2,1,0:T(8,128)(2,1)}, u32[]{:S(2)}, u32[]{:S(2)}) collective-permute-start(bf16[256,8,128]{2,1,0:T(8,128)(2,1)} %collective-permute-done.3), channel_id=1, source_target_pairs={{0,15},{1,0},{2,1},{3,2},{4,3},{5,4},{6,5},{7,6},{8,7},{9,8},{10,9... | collective-permute-start | bytes 1572872 | tf_op jit(solution)/shard_map/ppermute | solution.py:25
  58.6 19.7 %copy-start.5 = (bf16[256,8,128]{2,1,0:T(8,128)(2,1)S(1)}, bf16[256,8,128]{2,1,0:T(8,128)(2,1)}, u32[]{:S(2)}) copy-start(bf16[256,8,128]{2,1,0:T(8,128)(2,1)} %param.15) | copy-start | bytes 1572868
  64.5 14.8 %collective-permute-start.6 = (bf16[256,8,128]{2,1,0:T(8,128)(2,1)}, bf16[256,8,128]{2,1,0:T(8,128)(2,1)}, u32[]{:S(2)}, u32[]{:S(2)}) collective-permute-start(bf16[256,8,128]{2,1,0:T(8,128)(2,1)} %collective-permute-done.4), channel_id=1, source_target_pairs={{0,1},{1,2},{2,3},{3,4},{4,5},{5,6},{6,7},{7,8},{8,9},{9,10},{10,1... | collective-permute-start | bytes 1572872 | tf_op jit(solution)/shard_map/ppermute | solution.py:20
  67.8 14.0 %collective-permute-start.7 = (bf16[256,8,128]{2,1,0:T(8,128)(2,1)}, bf16[256,8,128]{2,1,0:T(8,128)(2,1)}, u32[]{:S(2)}, u32[]{:S(2)}) collective-permute-start(bf16[256,8,128]{2,1,0:T(8,128)(2,1)} %collective-permute-done.5), channel_id=1, source_target_pairs={{0,15},{1,0},{2,1},{3,2},{4,3},{5,4},{6,5},{7,6},{8,7},{9,8},{10,9... | collective-permute-start | bytes 1572872 | tf_op jit(solution)/shard_map/ppermute | solution.py:25
  79.3 14.2 %collective-permute-start.8 = (bf16[256,8,128]{2,1,0:T(8,128)(2,1)}, bf16[256,8,128]{2,1,0:T(8,128)(2,1)}, u32[]{:S(2)}, u32[]{:S(2)}) collective-permute-start(bf16[256,8,128]{2,1,0:T(8,128)(2,1)} %collective-permute-done.6), channel_id=1, source_target_pairs={{0,1},{1,2},{2,3},{3,4},{4,5},{5,6},{6,7},{7,8},{8,9},{9,10},{10,1... | collective-permute-start | bytes 1572872 | tf_op jit(solution)/shard_map/ppermute | solution.py:20
  81.9 23.3 %collective-permute-start.9 = (bf16[256,8,128]{2,1,0:T(8,128)(2,1)}, bf16[256,8,128]{2,1,0:T(8,128)(2,1)}, u32[]{:S(2)}, u32[]{:S(2)}) collective-permute-start(bf16[256,8,128]{2,1,0:T(8,128)(2,1)} %collective-permute-done.7), channel_id=1, source_target_pairs={{0,15},{1,0},{2,1},{3,2},{4,3},{5,4},{6,5},{7,6},{8,7},{9,8},{10,9... | collective-permute-start | bytes 1572872 | tf_op jit(solution)/shard_map/ppermute | solution.py:25
  93.4 18.9 %collective-permute-start.10 = (bf16[256,8,128]{2,1,0:T(8,128)(2,1)}, bf16[256,8,128]{2,1,0:T(8,128)(2,1)}, u32[]{:S(2)}, u32[]{:S(2)}) collective-permute-start(bf16[256,8,128]{2,1,0:T(8,128)(2,1)} %collective-permute-done.8), channel_id=1, source_target_pairs={{0,1},{1,2},{2,3},{3,4},{4,5},{5,6},{6,7},{7,8},{8,9},{9,10},{10,1... | collective-permute-start | bytes 1572872 | tf_op jit(solution)/shard_map/ppermute | solution.py:20
  99.4 42.9 %copy-start.4 = (bf16[256,256]{1,0:T(8,128)(2,1)S(1)}, bf16[256,256]{1,0:T(8,128)(2,1)}, u32[]{:S(2)}) copy-start(bf16[256,256]{1,0:T(8,128)(2,1)} %param.13) | copy-start | bytes 393220
  105.2 16.8 %collective-permute-start.11 = (bf16[256,8,128]{2,1,0:T(8,128)(2,1)}, bf16[256,8,128]{2,1,0:T(8,128)(2,1)S(1)}, u32[]{:S(2)}, u32[]{:S(2)}) collective-permute-start(bf16[256,8,128]{2,1,0:T(8,128)(2,1)} %collective-permute-done.9), channel_id=1, source_target_pairs={{0,15},{1,0},{2,1},{3,2},{4,3},{5,4},{6,5},{7,6},{8,7},{9,8},{10,9... | collective-permute-start | bytes 1572872 | tf_op jit(solution)/shard_map/ppermute | solution.py:25
  112.3 16.8 %collective-permute-start.12 = (bf16[256,8,128]{2,1,0:T(8,128)(2,1)}, bf16[256,8,128]{2,1,0:T(8,128)(2,1)S(1)}, u32[]{:S(2)}, u32[]{:S(2)}) collective-permute-start(bf16[256,8,128]{2,1,0:T(8,128)(2,1)} %collective-permute-done.10), channel_id=1, source_target_pairs={{0,1},{1,2},{2,3},{3,4},{4,5},{5,6},{6,7},{7,8},{8,9},{9,10},{10,1... | collective-permute-start | bytes 1572872 | tf_op jit(solution)/shard_map/ppermute | solution.py:20
  122.0 15.0 %collective-permute-start.13 = (bf16[256,8,128]{2,1,0:T(8,128)(2,1)S(1)}, bf16[256,8,128]{2,1,0:T(8,128)(2,1)S(1)}, u32[]{:S(2)}, u32[]{:S(2)}) collective-permute-start(bf16[256,8,128]{2,1,0:T(8,128)(2,1)S(1)} %collective-permute-done.11), channel_id=1, source_target_pairs={{0,15},{1,0},{2,1},{3,2},{4,3},{5,4},{6,5},{7,6},{8,7},{9,8},{10,9... | collective-permute-start | bytes 1572872 | tf_op jit(solution)/shard_map/ppermute | solution.py:25
  129.1 12.3 %collective-permute-start.14 = (bf16[256,8,128]{2,1,0:T(8,128)(2,1)S(1)}, bf16[256,8,128]{2,1,0:T(8,128)(2,1)S(1)}, u32[]{:S(2)}, u32[]{:S(2)}) collective-permute-start(bf16[256,8,128]{2,1,0:T(8,128)(2,1)S(1)} %collective-permute-done.12), channel_id=1, source_target_pairs={{0,1},{1,2},{2,3},{3,4},{4,5},{5,6},{6,7},{7,8},{8,9},{9,10},{10,1... | collective-permute-start | bytes 1572872 | tf_op jit(solution)/shard_map/ppermute | solution.py:20
  323.1 0.7 copy-start.1
  323.1 0.7 copy-start.6
  332.0 95.8 %all-to-all-start = ((bf16[32,2,1,2,8,128]{5,4,3,1,2,0:T(8,128)(2,1)}), bf16[32,2,1,2,8,128]{5,4,3,1,2,0:T(8,128)(2,1)}, u32[]{:S(2)}, u32[]{:S(2)}) async-start(bf16[32,2,1,2,8,128]{5,4,3,1,2,0:T(8,128)(2,1)} %bitcast.103), calls=%async_computation | async-start | bytes 524288 | tf_op jit(solution)/shard_map/all_to_all | solution.py:157
  393.3 0.8 copy-start.2
  425.8 0.8 copy-start.3
Sparse Core Ops, SparseCore 0:
  41.3 129.7 all-reduce.5
  324.9 93.3 all-gather.4
